TPU v7x, 512 devices: a whole 4x8x8 slice. The times are simulated.
512 devices in a mesh: seq: 32 (over x, z_lo, core), tp: 16 (over y, z_hi).
Axes of the slice: x: 4, y: 8, z: 8 (z_hi: 2, z_lo: 4; z = z_hi * 4 + z_lo), core: 2. Of those that a mesh axis runs over, the one named last changes fastest.
Arguments:
- q_in: bfloat16 [16384, 4096], P('seq', 'tp'), may hold values from -40 to 40
- k_in: bfloat16 [16384, 4096], P('seq', 'tp'), may hold values from -40 to 40
- v_in: bfloat16 [16384, 4096], P('seq', 'tp'), may hold values from -6 to 6
- q_gain: float32 [4096], P('tp'), may hold values from 0.1 to 1.9
- k_gain: float32 [4096], P('tp'), may hold values from 0.1 to 1.9
- d_out: bfloat16 [16384, 4096], P('seq', 'tp'), may hold values from -6 to 6
- counts: int32 [64], replicated, may hold values from 128 to 256, as said below
- windows: int32 [32], P('tp'), may hold values from 1 to 2
Outputs:
- attn_out: bfloat16 [16384, 4096], P('seq', 'tp')
- grad_q: bfloat16 [16384, 4096], P('seq', 'tp')
- grad_k: bfloat16 [16384, 4096], P('seq', 'tp')
- grad_v: bfloat16 [16384, 4096], P('seq', 'tp')
Inputs may be any that keep to these rules, and one draw needn't show every extreme that they name: `counts`: each count is a multiple of 128; slots at or beyond a frame's count are padding; some frame is full.
All inputs are finite; a program needn't handle non-finite values.
Results may differ from a plain program's by a relative error of at most 0.02.
The roundings to bfloat16 on the way count: a program that leaves them out, or rounds other values in their place, can miss the bound.
Values may be sent and summed in bfloat16 or wider, within the bound.
No kernel may reach another device: no remote copies, remote signals or barrier semaphores. Data moves between devices by JAX's collectives and lax.ppermute only.
A program may use at most 64 MiB of HBM per device.

v0:
```python
import jax
import jax.numpy as jnp
from jax import lax
from jax.sharding import PartitionSpec as P

HD = 128
CAP = 256
F_DEV = 2
WIDTH = 4096
EPS = 1e-06
NEG = -1e30


def shifted(block, axis, distance):
    devices = range(lax.axis_size(axis))
    route = [(i - distance, i) for i in devices if i - distance in devices]
    return lax.ppermute(block, axis, route)


def from_root(x, axis, root):
    mine = lax.axis_index(axis) == root
    return lax.psum(jnp.where(mine, x, jnp.zeros_like(x)), axis)


def stack_offsets(padded, before, count):
    blocks = [padded[before - offset : before - offset + count] for offset in range(before + 1)]
    return jnp.concatenate(blocks, axis=1)


def fold_offsets(grads, before, count, slots):
    result = jnp.zeros((before + count, slots) + grads.shape[2:], jnp.float32)
    for offset in range(before + 1):
        piece = grads[:, offset * slots : (offset + 1) * slots]
        result = result + jnp.pad(piece, ((before - offset, offset), (0, 0), (0, 0)))
    return result


def attend(q_head, g_head, k_set, v_set, visible, row_live):
    factor = HD ** (-0.5)
    scores = jnp.einsum("fqd,fkd->fqk", q_head, k_set, preferred_element_type=jnp.float32) * factor
    scores = jnp.where(visible[:, None, :], scores, NEG)
    row_max = jnp.max(scores, axis=2, keepdims=True)
    row_sum = jnp.sum(jnp.exp(scores - row_max), axis=2, keepdims=True)
    lse = row_max + jnp.log(row_sum)
    prob_wide = jnp.exp(scores - lse)
    prob = prob_wide.astype(jnp.bfloat16)
    out_wide = jnp.einsum("fqk,fkd->fqd", prob, v_set, preferred_element_type=jnp.float32)
    attn = lax.optimization_barrier(
        jnp.where(row_live[:, :, None], out_wide, 0.0).astype(jnp.bfloat16)
    )
    delta = jnp.sum(g_head.astype(jnp.float32) * attn.astype(jnp.float32), axis=2)
    dprob = jnp.einsum("fqd,fkd->fqk", g_head, v_set, preferred_element_type=jnp.float32)
    dscore = (prob_wide * (dprob - delta[:, :, None]) * factor).astype(jnp.bfloat16)
    grad_qh = jnp.einsum("fqk,fkd->fqd", dscore, k_set, preferred_element_type=jnp.float32)
    grad_kh = jnp.einsum("fqk,fqd->fkd", dscore, q_head, preferred_element_type=jnp.float32)
    grad_vh = jnp.einsum("fqk,fqd->fkd", prob, g_head, preferred_element_type=jnp.float32)
    return (attn, lse[:, :, 0], delta, grad_qh, grad_kh, grad_vh)


def on_device(q_in, k_in, v_in, q_gain, k_gain, d_out, counts, windows):
    row_count, local_width = q_in.shape
    local_heads = local_width // HD
    device = lax.axis_index("seq")
    q_float = q_in.astype(jnp.float32)
    k_float = k_in.astype(jnp.float32)
    q_power, k_power = lax.psum(
        (jnp.sum(q_float * q_float, axis=1), jnp.sum(k_float * k_float, axis=1)), "tp"
    )
    q_rinv = lax.rsqrt(q_power / WIDTH + EPS)[:, None]
    k_rinv = lax.rsqrt(k_power / WIDTH + EPS)[:, None]
    q_norm = (q_float * q_rinv * q_gain).astype(jnp.bfloat16)
    k_norm = (k_float * k_rinv * k_gain).astype(jnp.bfloat16)
    padded_counts = jnp.concatenate([jnp.zeros((F_DEV,), jnp.int32), counts])
    near_counts = lax.dynamic_slice_in_dim(padded_counts, device * F_DEV, 2 * F_DEV)
    slot_index = jnp.arange(CAP, dtype=jnp.int32)
    near_live = slot_index[None, :] < near_counts[:, None]
    row_live = near_live[F_DEV:]
    grad_mask = jnp.where(row_live.reshape(row_count)[:, None], d_out, jnp.zeros_like(d_out))
    halo_k, halo_v = shifted((k_norm, v_in), "seq", 1)
    anchor_k, anchor_v = (from_root(k_norm[:CAP], "seq", 0), from_root(v_in[:CAP], "seq", 0))
    k_near = jnp.concatenate([halo_k, k_norm], axis=0).reshape(2 * F_DEV, CAP, local_width)
    v_near = jnp.concatenate([halo_v, v_in], axis=0).reshape(2 * F_DEV, CAP, local_width)
    k_set = jnp.concatenate(
        [
            stack_offsets(k_near, F_DEV, F_DEV),
            jnp.broadcast_to(anchor_k[None], (F_DEV, CAP, local_width)),
        ],
        axis=1,
    )
    v_set = jnp.concatenate(
        [
            stack_offsets(v_near, F_DEV, F_DEV),
            jnp.broadcast_to(anchor_v[None], (F_DEV, CAP, local_width)),
        ],
        axis=1,
    )

    def to_heads(value):
        return value.reshape(value.shape[0], value.shape[1], local_heads, HD).transpose(2, 0, 1, 3)

    def from_heads(value):
        return value.transpose(1, 2, 0, 3).reshape(value.shape[1], value.shape[2], local_heads * HD)

    frame_local = jnp.arange(F_DEV, dtype=jnp.int32)
    offsets = jnp.arange((F_DEV + 1) * CAP, dtype=jnp.int32) // CAP
    live_stack = stack_offsets(near_live[:, :, None], F_DEV, F_DEV)[:, :, 0]
    reach = device * F_DEV + frame_local[:, None] - offsets[None, :] >= 0
    within = offsets[None, None, :] <= windows[:, None, None]
    anchor_ok = device * F_DEV + frame_local[None, :] - windows[:, None] > 0
    anchor_live = slot_index < counts[0]
    visible = jnp.concatenate(
        [(live_stack & reach)[None] & within, anchor_ok[:, :, None] & anchor_live[None, None, :]],
        axis=2,
    )

    def per_head(items):
        q_head, g_head, k_head, v_head, seen = items
        return attend(q_head, g_head, k_head, v_head, seen, row_live)

    q_heads = to_heads(q_norm.reshape(F_DEV, CAP, local_width))
    g_heads = to_heads(grad_mask.reshape(F_DEV, CAP, local_width))
    attn_h, lse_h, delta_h, grad_qh, grad_kh, grad_vh = lax.map(
        per_head, (q_heads, g_heads, to_heads(k_set), to_heads(v_set), visible)
    )
    attn_out = from_heads(attn_h).reshape(row_count, local_width)
    grad_qn = from_heads(grad_qh).reshape(row_count, local_width)
    grad_k_all = from_heads(grad_kh)
    grad_v_all = from_heads(grad_vh)
    split = (F_DEV + 1) * CAP
    grad_k_near = fold_offsets(grad_k_all[:, :split], F_DEV, F_DEV, CAP)
    grad_v_near = fold_offsets(grad_v_all[:, :split], F_DEV, F_DEV, CAP)
    grad_k_anchor = jnp.sum(grad_k_all[:, split:], axis=0)
    grad_v_anchor = jnp.sum(grad_v_all[:, split:], axis=0)
    back_k, back_v = shifted((grad_k_near[:F_DEV], grad_v_near[:F_DEV]), "seq", -1)
    grad_k_own = grad_k_near[F_DEV:] + back_k
    grad_v_own = grad_v_near[F_DEV:] + back_v
    anchor_gk, anchor_gv = lax.psum((grad_k_anchor, grad_v_anchor), "seq")
    first_device = device == 0
    grad_k_own = grad_k_own.at[0].add(jnp.where(first_device, anchor_gk, 0.0))
    grad_v_own = grad_v_own.at[0].add(jnp.where(first_device, anchor_gv, 0.0))
    q_scaled = grad_qn * q_gain
    k_scaled = grad_k_own.reshape(row_count, local_width) * k_gain
    q_dot, k_dot = lax.psum(
        (jnp.sum(q_float * q_scaled, axis=1), jnp.sum(k_float * k_scaled, axis=1)), "tp"
    )
    grad_q = (q_rinv * q_scaled - q_float * q_rinv**3 * q_dot[:, None] / WIDTH).astype(jnp.bfloat16)
    grad_k = (k_rinv * k_scaled - k_float * k_rinv**3 * k_dot[:, None] / WIDTH).astype(jnp.bfloat16)
    grad_v = grad_v_own.reshape(row_count, local_width).astype(jnp.bfloat16)
    return (attn_out, grad_q, grad_k, grad_v)


def solution(mesh):
    return jax.shard_map(
        on_device,
        mesh=mesh,
        in_specs=(
            P("seq", "tp"),
            P("seq", "tp"),
            P("seq", "tp"),
            P("tp"),
            P("tp"),
            P("seq", "tp"),
            P(),
            P("tp"),
        ),
        out_specs=(P("seq", "tp"), P("seq", "tp"), P("seq", "tp"), P("seq", "tp")),
        check_vma=False,
    )
```

profile of v0, /device:TPU:8, one launch (start us, length us, event | category | flops | bytes accessed | tf_op | source)
XLA Modules:
  0.0 734.2 jit_solution(7441168945927711885)
XLA Ops:
  7.3 1.2 fusion.29
  8.5 1.1 fusion.37
  9.6 56.1 %all-reduce.9 = (f32[512]{0:T(512)S(1)}, f32[512]{0:T(512)S(1)}) all-reduce(f32[512]{0:T(512)S(1)} %fusion.29, f32[512]{0:T(512)S(1)} %fusion.37), channel_id=1, replica_groups=mesh['seq'=32,'tp'=16] {'tp'}, use_global_device_ids=true, to_apply=%region_1.0 | all-reduce | flops 1024 | bytes 8192 | tf_op jit(solution)/shard_map/psum | solution.py:66
  65.6 1.1 fusion.39
  66.7 1.3 collective-permute-start
  68.1 4.0 collective-permute-start.1
  72.1 0.9 slice_select_fusion.1
  73.0 0.7 broadcast_in_dim.108
  73.7 0.7 broadcast_in_dim.110
  75.8 280.9 %all-reduce.16.cloned.1.call-done = (bf16[256,2,128]{2,1,0:T(2,128)(2,1)}, bf16[256,2,128]{2,1,0:T(2,128)(2,1)}) async-done(((bf16[256,2,128]{2,1,0:T(2,128)(2,1)}, bf16[256,2,128]{2,1,0:T(2,128)(2,1)}), (bf16[256,2,128]{2,1,0:T(2,128)(2,1)}, bf16[256,2,128]{2,1,0:T(2,128)(2,1)})) %all-reduce.16.cloned.1.call-update) | async-done | bytes 262160 | tf_op jit(solution)/shard_map/psum | solution.py:22
  356.7 0.9 copy.27
  357.8 0.7 copy.29
  358.6 0.7 copy.30
  359.7 1.6 maximum_bitcast_fusion.1
  361.5 17.1 %while.18 = (s32[]{:T(128)}, bf16[2,2,256,128]{3,2,1,0:T(8,128)(2,1)}, f32[2,2,256,128]{3,2,1,0:T(8,128)}, f32[2,2,1024,128]{3,2,1,0:T(8,128)}, f32[2,2,1024,128...) while((s32[]{:T(128)}, ...), condition=%wide.region_10.11_spmd, body=%wide.region_6.10_spmd.sunk | while | flops 813038592 | bytes 57053992 | solution.py:122
  361.6 0.5 fusion.82
  362.1 0.5 exponential_reduce_fusion.2
  362.7 0.5 copy-done.5
  363.2 0.7 fusion.86
  363.9 1.3 copy-done.6
  365.2 0.5 fusion.83
  365.8 0.2 multiply_reduce_fusion.2
  365.9 0.6 multiply_convert_fusion.2
  366.6 0.8 copy-done.2
  367.3 0.5 fusion.85
  367.9 0.4 fusion.84
  368.4 0.9 copy-done.3
  369.2 0.7 bitcast_dynamic-update-slice_fusion.2
  369.9 0.2 copy-done.11
  370.1 0.5 fusion.82
  370.6 0.5 exponential_reduce_fusion.2
  371.1 0.5 copy-done.5
  371.7 0.7 fusion.86
  372.4 1.3 copy-done.6
  373.7 0.5 fusion.83
  374.3 0.2 multiply_reduce_fusion.2
  374.4 0.6 multiply_convert_fusion.2
  375.1 0.8 copy-done.2
  375.9 0.5 fusion.85
  376.4 0.4 fusion.84
  376.9 0.9 copy-done.3
  377.8 0.7 bitcast_dynamic-update-slice_fusion.2
  378.5 0.2 copy-done.11
  378.6 1.7 copy_bitcast_fusion
  380.4 0.8 fusion.52
  381.3 0.8 slice.172
  382.1 1.3 collective-permute-start.3
  383.4 0.2 copy_bitcast_fusion.1
  383.6 1.6 slice_reduce_fusion.1
  385.3 1.2 pad_add_fusion.1
  386.5 0.8 slice.165
  387.3 1.3 collective-permute-start.2
  388.6 0.4 copy.34
  389.0 0.2 fusion.36
  389.2 1.2 copy.33
  390.4 0.7 copy.52
  391.2 1.1 slice_add_fusion
  392.3 277.9 %all-reduce.14.cloned.1.call-done = (f32[256,256]{1,0:T(8,128)}, f32[256,256]{1,0:T(8,128)}) async-done(((f32[256,256]{1,0:T(8,128)}, f32[256,256]{1,0:T(8,128)}), (f32[256,256]{1,0:T(8,128)}, f32[256,256]{1,0:T(8,128)})) %all-reduce.14.cloned.1.call-update) | async-done | bytes 524304 | tf_op jit(solution)/shard_map/psum | solution.py:137
  670.2 1.1 fusion.45
  671.2 0.7 convert_element_type.54
  672.0 1.1 slice_add_fusion.1
  673.3 52.0 %all-reduce.8 = (f32[512]{0:T(512)S(1)}, f32[512]{0:T(512)S(1)}) all-reduce(f32[512]{0:T(512)S(1)} %fusion.36, f32[512]{0:T(512)S(1)} %fusion.44), channel_id=1, replica_groups=mesh['seq'=32,'tp'=16] {'tp'}, use_global_device_ids=true, to_apply=%region_12.13 | all-reduce | flops 1024 | bytes 8192 | tf_op jit(solution)/shard_map/psum | solution.py:143
  725.4 1.0 fusion.43
  726.3 1.0 fusion.35
  (94 shorter events, 2.4 us)
Async XLA Ops:
  7.2 67.9 %copy-start.1 = (bf16[512,256]{1,0:T(8,128)(2,1)S(1)}, bf16[512,256]{1,0:T(8,128)(2,1)}, u32[]{:S(2)}) copy-start(bf16[512,256]{1,0:T(8,128)(2,1)} %param.14) | copy-start | bytes 786436
  7.2 68.2 %copy-start.7 = (bf16[512,256]{1,0:T(8,128)(2,1)S(1)}, bf16[512,256]{1,0:T(8,128)(2,1)}, u32[]{:S(2)}) copy-start(bf16[512,256]{1,0:T(8,128)(2,1)} %param.16) | copy-start | bytes 786436
  7.2 67.3 %copy-start.19 = (s32[64]{0:T(128)S(1)}, s32[64]{0:T(128)}, u32[]{:S(2)}) copy-start(s32[64]{0:T(128)} %param.20) | copy-start | bytes 772
  7.2 67.6 %copy-start.18 = (s32[2]{0:T(128)S(1)}, s32[2]{0:T(128)}, u32[]{:S(2)}) copy-start(s32[2]{0:T(128)} %param.21) | copy-start | bytes 28
  7.2 67.7 %copy-start.13 = (bf16[512,256]{1,0:T(8,128)(2,1)S(1)}, bf16[512,256]{1,0:T(8,128)(2,1)}, u32[]{:S(2)}) copy-start(bf16[512,256]{1,0:T(8,128)(2,1)} %param.19) | copy-start | bytes 786436
  7.2 67.9 %copy-start.17 = (f32[256]{0:T(256)S(1)}, f32[256]{0:T(256)}, u32[]{:S(2)}) copy-start(f32[256]{0:T(256)} %param.17) | copy-start | bytes 3076
  7.2 349.5 %all-reduce.16.cloned.1.call-start = ((), (), s32[]{:S(2)}) async-start(), calls=%async_computation.1 | async-start | bytes 524288 | tf_op jit(solution)/shard_map/psum | solution.py:22
  66.7 290.9 %collective-permute-start = (bf16[512,256]{1,0:T(8,128)(2,1)S(1)}, bf16[512,256]{1,0:T(8,128)(2,1)S(1)}, u32[]{:S(2)}, u32[]{:S(2)}) collective-permute-start(bf16[512,256]{1,0:T(8,128)(2,1)S(1)} %fusion.39), channel_id=1, source_target_pairs={{0,16},{16,32},{32,48},{48,64},{64,80},{80,96},{96,112},{112,128},... | collective-permute-start | bytes 786440 | tf_op jit(solution)/shard_map/ppermute | solution.py:17
  68.1 291.3 %collective-permute-start.1 = (bf16[512,256]{1,0:T(8,128)(2,1)}, bf16[512,256]{1,0:T(8,128)(2,1)S(1)}, u32[]{:S(2)}, u32[]{:S(2)}) collective-permute-start(bf16[512,256]{1,0:T(8,128)(2,1)} %param.16), channel_id=1, source_target_pairs={{0,16},{16,32},{32,48},{48,64},{64,80},{80,96},{96,112},{112,128},... | collective-permute-start | bytes 786440 | tf_op jit(solution)/shard_map/ppermute | solution.py:17
  74.4 595.7 %all-reduce.14.cloned.1.call-start = ((), (), s32[]{:S(2)}) async-start(), calls=%async_computation | async-start | bytes 1048576 | tf_op jit(solution)/shard_map/psum | solution.py:137
  357.7 1.8 copy-start.15
  359.6 1.8 copy-start.8
  359.7 1.8 copy-start.9
  361.6 1.6 copy-start.5
  363.9 1.3 copy-start.6
  365.8 1.6 copy-start.2
  365.9 2.0 copy-start.10
  367.9 1.3 copy-start.3
  369.2 0.9 copy-start.11
  370.1 1.6 copy-start.5
  372.4 1.3 copy-start.6
  374.3 1.6 copy-start.2
  374.4 2.0 copy-start.10
  376.4 1.3 copy-start.3
  377.7 0.9 copy-start.11
  381.2 2.2 copy-start.4
  382.1 9.0 %collective-permute-start.3 = (f32[2,256,256]{2,1,0:T(8,128)}, f32[2,256,256]{2,1,0:T(8,128)}, u32[]{:S(2)}, u32[]{:S(2)}) collective-permute-start(f32[2,256,256]{2,1,0:T(8,128)} %slice.172), channel_id=1, source_target_pairs={{16,0},{32,16},{48,32},{64,48},{80,64},{96,80},{112,96},{128,112},... | collective-permute-start | bytes 1572872 | tf_op jit(solution)/shard_map/ppermute | solution.py:17
  385.3 3.3 copy-start.12
  387.3 284.6 %collective-permute-start.2 = (f32[2,256,256]{2,1,0:T(8,128)}, f32[2,256,256]{2,1,0:T(8,128)}, u32[]{:S(2)}, u32[]{:S(2)}) collective-permute-start(f32[2,256,256]{2,1,0:T(8,128)} %slice.165), channel_id=1, source_target_pairs={{16,0},{32,16},{48,32},{64,48},{80,64},{96,80},{112,96},{128,112},... | collective-permute-start | bytes 1572872 | tf_op jit(solution)/shard_map/ppermute | solution.py:17
  392.3 280.9 %copy-start = (bf16[512,256]{1,0:T(8,128)(2,1)S(1)}, bf16[512,256]{1,0:T(8,128)(2,1)}, u32[]{:S(2)}) copy-start(bf16[512,256]{1,0:T(8,128)(2,1)} %param.15) | copy-start | bytes 786436
  392.3 280.9 %copy-start.16 = (f32[256]{0:T(256)S(1)}, f32[256]{0:T(256)}, u32[]{:S(2)}) copy-start(f32[256]{0:T(256)} %param.18) | copy-start | bytes 3076
  670.2 2.9 copy-start.14
Sparse Core Ops, SparseCore 0:
  74.6 282.1 all-reduce.15
  385.4 284.7 all-reduce.13
where the time goes:
time: 735 us; the launch traced here: 734 us
  waiting for transfers between devices  559 us (76%)
  blocking collectives  108 us (15%)
  local copies, waits for them, and re-layouts  19.6 us (3%)
  other arithmetic  18.1 us (2%)
  between operations  14.6 us (2%)
  starting transfers between devices  7.95 us (1%)
    psum x1, waiting for transfers between devices, from_root(): return lax.psum(jnp.where(mine, x, jnp.zeros_like(x)), axis)  281 us
    psum x1, waiting for transfers between devices, on_device(): anchor_gk, anchor_gv = lax.psum((grad_k_anchor, grad_v_anchor), 'seq')  278 us
    psum x1, blocking collectives, on_device(): lax.psum((jnp.sum(q_float * q_float, axis=1), jnp.sum(k_float * k_float,...  56.1 us
    psum x1, blocking collectives, on_device(): lax.psum((jnp.sum(q_float * q_scaled, axis=1), jnp.sum(k_float * k_scaled...  52 us
  transfers between devices with their start and end apart: 6, of which 2 were waited for; matrix products, arithmetic and copies ran while one was open for 2% of the time, Pallas kernels for 0%

commit v1 on v0

--- a/solution.py
+++ b/solution.py
@@ -2,6 +2,7 @@
 import jax.numpy as jnp
 from jax import lax
 from jax.sharding import PartitionSpec as P
+from jax.lax import all_gather
 
 HD = 128
 CAP = 256
@@ -19,7 +20,11 @@
 
 def from_root(x, axis, root):
     mine = lax.axis_index(axis) == root
-    return lax.psum(jnp.where(mine, x, jnp.zeros_like(x)), axis)
+
+    def proceed_quotas_on_mesh(xs):
+        return jnp.sum(all_gather(xs, axis), 0)
+
+    return proceed_quotas_on_mesh(jnp.where(mine, x, jnp.zeros_like(x)))
 
 
 def stack_offsets(padded, before, count):

time: 735 us -> 578 us (0.79)
  waiting for transfers between devices: 559 us -> 395 us
  other arithmetic: 18.1 us -> 26.9 us
    psum x1 -> x0, waiting for transfers between devices: 281 us -> none  [from_root(): return lax.psum(jnp.where(mine, x, jnp.zeros_like(x)), axis)]
    all_gather x0 -> x2, waiting for transfers between devices: none -> 114 us  [proceed_quotas_on_mesh(): return jnp.sum(all_gather(xs, axis), 0)]
  transfers between devices with their start and end apart: 6 -> 7, of which waited for: 2 -> 3; matrix products, arithmetic and copies ran while one was open for 2% -> 3% of each run, Pallas kernels for 0% -> 0%
where the time goes in v1:
time: 578 us; the launch traced here: 577 us
  waiting for transfers between devices  395 us (68%)
  blocking collectives  108 us (19%)
  other arithmetic  26.9 us (5%)
  local copies, waits for them, and re-layouts  18.2 us (3%)
  between operations  14.3 us (2%)
  starting transfers between devices  7.99 us (1%)
  matrix products  6.8 us (1%)
    psum x1, waiting for transfers between devices, on_device(): anchor_gk, anchor_gv = lax.psum((grad_k_anchor, grad_v_anchor), 'seq')  281 us
    all_gather x2, waiting for transfers between devices, proceed_quotas_on_mesh(): return jnp.sum(all_gather(xs, axis), 0)  114 us
    psum x1, blocking collectives, on_device(): lax.psum((jnp.sum(q_float * q_float, axis=1), jnp.sum(k_float * k_float,...  56.1 us
    psum x1, blocking collectives, on_device(): lax.psum((jnp.sum(q_float * q_scaled, axis=1), jnp.sum(k_float * k_scaled...  52 us
  transfers between devices with their start and end apart: 7, of which 3 were waited for; matrix products, arithmetic and copies ran while one was open for 3% of the time, Pallas kernels for 0%

profile of v1, /device:TPU:8, one launch (start us, length us, event | category | flops | bytes accessed | tf_op | source)
XLA Modules:
  0.0 577.4 jit_solution(4119475487103086638)
XLA Ops:
  7.3 1.2 fusion.29
  8.4 1.1 fusion.37
  9.5 56.1 %all-reduce.9 = (f32[512]{0:T(512)S(1)}, f32[512]{0:T(512)S(1)}) all-reduce(f32[512]{0:T(512)S(1)} %fusion.29, f32[512]{0:T(512)S(1)} %fusion.37), channel_id=1, replica_groups=mesh['seq'=32,'tp'=16] {'tp'}, use_global_device_ids=true, to_apply=%region_1.0 | all-reduce | flops 1024 | bytes 8192 | tf_op jit(solution)/shard_map/psum | solution.py:71
  65.6 1.1 fusion.39
  66.7 0.7 slice_select_fusion
  67.4 1.6 slice_select_fusion.1
  69.1 1.3 collective-permute-start
  70.4 4.0 collective-permute-start.1
  74.4 0.7 pad_dynamic-slice_fusion
  75.3 0.7 iota_compare_fusion.1
  75.9 0.7 subtract_compare_fusion
  76.7 0.7 fusion.47
  78.4 0.7 copy.42
  79.2 0.7 copy.43
  80.1 51.0 %all-gather.5.cloned.1.call-done = bf16[8192,256]{1,0:T(8,128)(2,1)} async-done(((bf16[256,256]{1,0:T(8,128)(2,1)}), bf16[8192,256]{1,0:T(8,128)(2,1)}) %all-gather.5.cloned.1.call-update) | async-done | bytes 4194320 | tf_op jit(solution)/shard_map/all_gather | solution.py:25
  131.1 2.8 reduce_sum.98
  134.1 63.3 %all-gather.7.cloned.1.call-done = bf16[8192,256]{1,0:T(8,128)(2,1)} async-done(((bf16[256,256]{1,0:T(8,128)(2,1)}), bf16[8192,256]{1,0:T(8,128)(2,1)}) %all-gather.7.cloned.1.call-update) | async-done | bytes 4194320 | tf_op jit(solution)/shard_map/all_gather | solution.py:25
  197.4 2.8 reduce_sum.99
  200.6 1.6 maximum_bitcast_fusion.1
  202.5 0.7 copy-done.14
  203.2 17.1 %while.18 = (s32[]{:T(128)}, bf16[2,2,256,128]{3,2,1,0:T(8,128)(2,1)S(1)}, f32[2,2,256,128]{3,2,1,0:T(8,128)}, f32[2,2,1024,128]{3,2,1,0:T(8,128)}, f32[2,2,1024...) while((s32[]{:T(128)}, ...), condition=%wide.region_10.11_spmd, body=%wide.region_6.10_spmd.sunk | while | flops 813038592 | bytes 57053484 | solution.py:127
  203.2 0.5 fusion.82
  203.7 0.5 exponential_reduce_fusion.2
  204.2 0.5 copy-done.5
  204.8 0.7 fusion.86
  205.5 1.3 copy-done.6
  206.8 0.5 fusion.83
  207.5 0.6 multiply_convert_fusion.2
  208.2 0.8 copy-done.2
  208.9 0.5 fusion.85
  209.5 0.4 fusion.84
  209.9 0.9 copy-done.3
  210.9 0.8 copy-done.11
  211.7 0.5 fusion.82
  212.3 0.5 exponential_reduce_fusion.2
  212.8 0.5 copy-done.5
  213.3 0.7 fusion.86
  214.1 1.3 copy-done.6
  215.4 0.5 fusion.83
  216.1 0.6 multiply_convert_fusion.2
  216.7 0.8 copy-done.2
  217.5 0.5 fusion.85
  218.1 0.4 fusion.84
  218.5 0.9 copy-done.3
  219.4 0.8 copy-done.11
  220.3 1.8 copy_bitcast_fusion
  222.1 0.8 fusion.52
  223.1 0.9 slice.172
  223.9 1.3 collective-permute-start.3
  225.4 1.6 slice_reduce_fusion.1
  227.1 1.2 pad_add_fusion.1
  228.3 0.8 slice.165
  229.1 1.3 collective-permute-start.2
  230.4 0.4 copy.49
  231.0 0.3 copy.48
  231.3 0.7 copy.67
  232.0 1.1 slice_add_fusion
  233.2 280.5 %all-reduce.12.cloned.1.call-done = (f32[256,256]{1,0:T(8,128)}, f32[256,256]{1,0:T(8,128)}) async-done(((f32[256,256]{1,0:T(8,128)}, f32[256,256]{1,0:T(8,128)}), (f32[256,256]{1,0:T(8,128)}, f32[256,256]{1,0:T(8,128)})) %all-reduce.12.cloned.1.call-update) | async-done | bytes 524304 | tf_op jit(solution)/shard_map/psum | solution.py:142
  513.7 1.1 fusion.45
  514.8 0.7 convert_element_type.58
  515.5 1.1 slice_add_fusion.1
  516.9 52.0 %all-reduce.8 = (f32[512]{0:T(512)S(1)}, f32[512]{0:T(512)S(1)}) all-reduce(f32[512]{0:T(512)S(1)} %fusion.36, f32[512]{0:T(512)S(1)} %fusion.44), channel_id=1, replica_groups=mesh['seq'=32,'tp'=16] {'tp'}, use_global_device_ids=true, to_apply=%region_12.13 | all-reduce | flops 1024 | bytes 8192 | tf_op jit(solution)/shard_map/psum | solution.py:148
  568.9 1.0 fusion.43
  569.9 1.0 fusion.35
  (100 shorter events, 3.3 us)
Async XLA Ops:
  7.2 70.4 %copy-start.1 = (bf16[512,256]{1,0:T(8,128)(2,1)S(1)}, bf16[512,256]{1,0:T(8,128)(2,1)}, u32[]{:S(2)}) copy-start(bf16[512,256]{1,0:T(8,128)(2,1)} %param.14) | copy-start | bytes 786436
  7.2 70.7 %copy-start.7 = (bf16[512,256]{1,0:T(8,128)(2,1)S(1)}, bf16[512,256]{1,0:T(8,128)(2,1)}, u32[]{:S(2)}) copy-start(bf16[512,256]{1,0:T(8,128)(2,1)} %param.16) | copy-start | bytes 786436
  7.2 70.2 %copy-start.13 = (bf16[512,256]{1,0:T(8,128)(2,1)S(1)}, bf16[512,256]{1,0:T(8,128)(2,1)}, u32[]{:S(2)}) copy-start(bf16[512,256]{1,0:T(8,128)(2,1)} %param.19) | copy-start | bytes 786436
  7.2 70.4 %copy-start.19 = (f32[256]{0:T(256)S(1)}, f32[256]{0:T(256)}, u32[]{:S(2)}) copy-start(f32[256]{0:T(256)} %param.17) | copy-start | bytes 3076
  7.2 123.9 %all-gather.5.cloned.1.call-start = ((), (), s32[]{:S(2)}) async-start(), calls=%async_computation | async-start | bytes 4325376 | tf_op jit(solution)/shard_map/all_gather | solution.py:25
  67.4 130.0 %all-gather.7.cloned.1.call-start = ((), (), s32[]{:S(2)}) async-start(), calls=%async_computation.1 | async-start | bytes 4325376 | tf_op jit(solution)/shard_map/all_gather | solution.py:25
  69.0 444.7 %all-reduce.12.cloned.1.call-start = ((), (), s32[]{:S(2)}) async-start(), calls=%async_computation.2 | async-start | bytes 1048576 | tf_op jit(solution)/shard_map/psum | solution.py:142
  69.1 9.2 %collective-permute-start = (bf16[512,256]{1,0:T(8,128)(2,1)S(1)}, bf16[512,256]{1,0:T(8,128)(2,1)S(1)}, u32[]{:S(2)}, u32[]{:S(2)}) collective-permute-start(bf16[512,256]{1,0:T(8,128)(2,1)S(1)} %fusion.39), channel_id=1, source_target_pairs={{0,16},{16,32},{32,48},{48,64},{64,80},{80,96},{96,112},{112,128},... | collective-permute-start | bytes 786440 | tf_op jit(solution)/shard_map/ppermute | solution.py:18
  70.4 9.6 %collective-permute-start.1 = (bf16[512,256]{1,0:T(8,128)(2,1)}, bf16[512,256]{1,0:T(8,128)(2,1)S(1)}, u32[]{:S(2)}, u32[]{:S(2)}) collective-permute-start(bf16[512,256]{1,0:T(8,128)(2,1)} %param.16), channel_id=1, source_target_pairs={{0,16},{16,32},{32,48},{48,64},{64,80},{80,96},{96,112},{112,128},... | collective-permute-start | bytes 786440 | tf_op jit(solution)/shard_map/ppermute | solution.py:18
  200.6 1.8 copy-start.8
  200.6 1.8 copy-start.9
  202.2 1.0 copy-start.14
  203.2 1.6 copy-start.5
  205.5 1.3 copy-start.6
  207.3 1.6 copy-start.2
  207.5 2.0 copy-start.10
  209.5 1.4 copy-start.3
  210.9 0.8 copy-start.11
  211.7 1.6 copy-start.5
  214.0 1.3 copy-start.6
  215.9 1.6 copy-start.2
  216.1 2.0 copy-start.10
  218.0 1.4 copy-start.3
  219.4 0.8 copy-start.11
  220.3 1.9 copy-start.15
  223.0 2.2 copy-start.4
  223.9 8.1 %collective-permute-start.3 = (f32[2,256,256]{2,1,0:T(8,128)}, f32[2,256,256]{2,1,0:T(8,128)}, u32[]{:S(2)}, u32[]{:S(2)}) collective-permute-start(f32[2,256,256]{2,1,0:T(8,128)} %slice.172), channel_id=1, source_target_pairs={{16,0},{32,16},{48,32},{64,48},{80,64},{96,80},{112,96},{128,112},... | collective-permute-start | bytes 1572872 | tf_op jit(solution)/shard_map/ppermute | solution.py:18
  227.1 3.4 copy-start.12
  228.3 2.7 copy-start.16
  229.1 286.3 %collective-permute-start.2 = (f32[2,256,256]{2,1,0:T(8,128)}, f32[2,256,256]{2,1,0:T(8,128)}, u32[]{:S(2)}, u32[]{:S(2)}) collective-permute-start(f32[2,256,256]{2,1,0:T(8,128)} %slice.165), channel_id=1, source_target_pairs={{16,0},{32,16},{48,32},{64,48},{80,64},{96,80},{112,96},{128,112},... | collective-permute-start | bytes 1572872 | tf_op jit(solution)/shard_map/ppermute | solution.py:18
  233.2 283.5 %copy-start = (bf16[512,256]{1,0:T(8,128)(2,1)S(1)}, bf16[512,256]{1,0:T(8,128)(2,1)}, u32[]{:S(2)}) copy-start(bf16[512,256]{1,0:T(8,128)(2,1)} %param.15) | copy-start | bytes 786436
  233.2 283.5 %copy-start.18 = (f32[256]{0:T(256)S(1)}, f32[256]{0:T(256)}, u32[]{:S(2)}) copy-start(f32[256]{0:T(256)} %param.18) | copy-start | bytes 3076
  513.7 2.9 copy-start.17
Sparse Core Ops, SparseCore 0:
  67.5 63.5 all-gather.4
  133.3 64.1 all-gather.6
  227.2 286.4 all-reduce.11
